TPU v7x, 32 devices: a whole 2x2x4 slice. The times are simulated.
32 devices in a mesh: ctx: 16 (over z, y, core), head: 2 (over x).
Axes of the slice: x: 2, y: 2, z: 4, core: 2. Of those that a mesh axis runs over, the one named last changes fastest.
Arguments:
- queries: bfloat16 [2048, 1536], P('ctx', 'head'), may hold values from -45 to 45
- key_rows: bfloat16 [2048, 256], P('ctx', 'head'), may hold values from -5 to 5
- value_rows: bfloat16 [2048, 256], P('ctx', 'head'), may hold values from -18 to 18
- cotangent: bfloat16 [2048, 1536], P('ctx', 'head'), may hold values from -6 to 6
- trace_ids: int32 [2048], P('ctx'), may hold values from 0 to 15, never falling along the last dimension, each value on 1 to 512 neighbouring positions
- correct: int32 [16], replicated, may hold values from 0 to 16, as said below
- group_size: int32 [16], replicated, may hold values from 4 to 16
Outputs:
- log_totals: float32 [2048, 12], P('ctx', 'head')
- grad_queries: float32 [2048, 1536], P('ctx', 'head')
- grad_keys: bfloat16 [2048, 256], P('ctx', 'head')
- grad_values: bfloat16 [2048, 256], P('ctx', 'head')
Inputs may be any that keep to these rules, and one draw needn't show every extreme that they name: correct[g] is at most group_size[g].
All inputs are finite; a program needn't handle non-finite values.
Results may differ from a plain program's by a relative error of at most 0.0054.
Values may be sent and summed in bfloat16 or wider, within the bound.
No kernel may reach another device: no remote copies, remote signals or barrier semaphores. Data moves between devices by JAX's collectives and lax.ppermute only.
A program may use at most 64 MiB of HBM per device.

v0:
```python
import math
import jax
import jax.numpy as jnp
from jax import lax
from jax.sharding import PartitionSpec as P

PASSK = 4


def pass_rate(correct, group_size):
    counts = group_size.astype(jnp.float32)
    hit_counts = correct.astype(jnp.float32)
    product = jnp.ones_like(counts)
    for offset in range(PASSK):
        product = product * (counts - hit_counts - offset) / (counts - offset)
    return 1.0 - product


def body(queries, key_rows, value_rows, cotangent, trace_ids, correct, group_size):
    tok_rows = queries.shape[0]
    half_rows = tok_rows // 2
    row_width = queries.shape[1]
    head_dim = key_rows.shape[1]
    head_count = row_width // head_dim
    ctx_count = lax.axis_size("ctx")
    my_index = lax.axis_index("ctx")
    length = tok_rows * ctx_count
    score_scale = 1.0 / math.sqrt(head_dim)
    pass_rates = pass_rate(correct, group_size)
    traces = jnp.arange(pass_rates.shape[0], dtype=jnp.int32)
    weights = jnp.sum(
        jnp.where(trace_ids[:, None] == traces[None, :], pass_rates[None, :], 0.0), axis=1
    )
    out_grads = (weights[:, None] * cotangent.astype(jnp.float32)).astype(jnp.bfloat16)
    first_base = my_index * tok_rows
    second_base = first_base + half_rows
    local_pos = jnp.arange(half_rows, dtype=jnp.int32)
    positions = jnp.concatenate([first_base + local_pos, second_base + local_pos], 0)
    last_first = first_base + half_rows - 1
    last_second = second_base + half_rows - 1
    query_all = queries.reshape(tok_rows, head_count, head_dim)
    grad_all = out_grads.reshape(tok_rows, head_count, head_dim)

    def run_block(running, key_block, value_block, key_start, block_fn):
        need_first = (key_start <= last_first).astype(jnp.int32)
        need_second = (key_start <= last_second).astype(jnp.int32)
        branch_index = need_first + 2 * need_second

        def skip_block(values_in):
            return values_in

        def first_only(values_in):
            return block_fn((0, half_rows), values_in, key_block, value_block, key_start)

        def second_only(values_in):
            return block_fn((half_rows, tok_rows), values_in, key_block, value_block, key_start)

        def both_halves(values_in):
            return block_fn((0, tok_rows), values_in, key_block, value_block, key_start)

        return lax.switch(branch_index, [skip_block, first_only, second_only, both_halves], running)

    def forward_block(row_span, running, key_block, value_block, key_start):
        row_begin, row_end = row_span
        row_peak, row_total, weighted = running
        query_part = query_all[row_begin:row_end]
        grad_part = grad_all[row_begin:row_end]
        query_pos = positions[row_begin:row_end]
        scores = (
            jnp.einsum("tqd,kd->tqk", query_part, key_block, preferred_element_type=jnp.float32)
            * score_scale
        )
        key_pos = key_start + jnp.arange(key_block.shape[0], dtype=jnp.int32)
        visible = key_pos[None, None, :] <= query_pos[:, None, None]
        block_peak = jnp.max(jnp.where(visible, scores, -1e30), axis=2)
        old_peak = row_peak[row_begin:row_end]
        new_peak = jnp.maximum(old_peak, block_peak)
        exp_terms = jnp.where(visible, jnp.exp(scores - new_peak[:, :, None]), 0.0)
        grad_probs = jnp.einsum(
            "tqd,kd->tqk", grad_part, value_block, preferred_element_type=jnp.float32
        )
        shrink = jnp.exp(old_peak - new_peak)
        new_total = row_total[row_begin:row_end] * shrink + jnp.sum(exp_terms, axis=2)
        new_weighted = weighted[row_begin:row_end] * shrink + jnp.sum(
            exp_terms * grad_probs, axis=2
        )
        return (
            row_peak.at[row_begin:row_end].set(new_peak),
            row_total.at[row_begin:row_end].set(new_total),
            weighted.at[row_begin:row_end].set(new_weighted),
        )

    row_peak = jnp.full((tok_rows, head_count), -1e30, jnp.float32)
    row_total = jnp.zeros((tok_rows, head_count), jnp.float32)
    weighted = jnp.zeros((tok_rows, head_count), jnp.float32)
    key_piece = lax.all_gather(key_rows, "ctx", axis=0, tiled=True)
    value_piece = lax.all_gather(value_rows, "ctx", axis=0, tiled=True)
    piece_rows = key_piece.shape[0]
    block_rows = math.gcd(piece_rows, 512)

    def forward_step(step_index, statistics):
        offset = step_index * block_rows
        key_block = lax.dynamic_slice_in_dim(key_piece, offset, block_rows, 0)
        value_block = lax.dynamic_slice_in_dim(value_piece, offset, block_rows, 0)
        return run_block(statistics, key_block, value_block, offset, forward_block)

    statistics = lax.fori_loop(
        0, piece_rows // block_rows, forward_step, (row_peak, row_total, weighted)
    )
    folded = statistics + (key_piece, value_piece)
    row_peak, row_total, weighted, key_store, value_store = folded
    log_totals = row_peak + jnp.log(row_total)
    delta_rows = weighted / row_total

    def backward_block(row_span, running, key_block, value_block, key_start):
        row_begin, row_end = row_span
        grad_query, zero_block = running
        query_part = query_all[row_begin:row_end]
        grad_part = grad_all[row_begin:row_end]
        query_pos = positions[row_begin:row_end]
        scores = (
            jnp.einsum("tqd,kd->tqk", query_part, key_block, preferred_element_type=jnp.float32)
            * score_scale
        )
        key_pos = key_start + jnp.arange(key_block.shape[0], dtype=jnp.int32)
        visible = key_pos[None, None, :] <= query_pos[:, None, None]
        probabilities = jnp.where(
            visible, jnp.exp(scores - log_totals[row_begin:row_end][:, :, None]), 0.0
        )
        prob_bf16 = probabilities.astype(jnp.bfloat16)
        grad_probs = jnp.einsum(
            "tqd,kd->tqk", grad_part, value_block, preferred_element_type=jnp.float32
        )
        grad_scores = (
            probabilities * (grad_probs - delta_rows[row_begin:row_end][:, :, None])
        ).astype(jnp.bfloat16)
        query_add = (
            jnp.einsum("tqk,kd->tqd", grad_scores, key_block, preferred_element_type=jnp.float32)
            * score_scale
        )
        key_add = (
            jnp.einsum("tqk,tqd->kd", grad_scores, query_part, preferred_element_type=jnp.float32)
            * score_scale
        )
        value_add = jnp.einsum(
            "tqk,tqd->kd", prob_bf16, grad_part, preferred_element_type=jnp.float32
        )
        return (
            grad_query.at[row_begin:row_end].add(query_add),
            jnp.concatenate([key_add, value_add], 1),
        )

    query_zero = jnp.zeros((tok_rows, head_count, head_dim), jnp.float32)
    key_block_rows = math.gcd(length, 512)

    def backward_step(step_index, running):
        grad_query, partial_sums = running
        key_start = step_index * key_block_rows
        key_block = lax.dynamic_slice_in_dim(key_store, key_start, key_block_rows, 0)
        value_block = lax.dynamic_slice_in_dim(value_store, key_start, key_block_rows, 0)
        zero_block = jnp.zeros((key_block_rows, 2 * head_dim), jnp.float32)
        grad_query, block_sums = run_block(
            (grad_query, zero_block), key_block, value_block, key_start, backward_block
        )
        partial_sums = lax.dynamic_update_slice_in_dim(partial_sums, block_sums, key_start, 0)
        return (grad_query, partial_sums)

    grad_query, partial_sums = lax.fori_loop(
        0,
        length // key_block_rows,
        backward_step,
        (query_zero, jnp.zeros((length, 2 * head_dim), jnp.float32)),
    )
    reduced = jnp.sum(
        lax.all_to_all(
            partial_sums.reshape(ctx_count, tok_rows, 2 * head_dim),
            "ctx",
            split_axis=0,
            concat_axis=0,
            tiled=True,
        ),
        axis=0,
    )
    grad_keys = reduced[:, :head_dim].astype(jnp.bfloat16)
    grad_values = reduced[:, head_dim:].astype(jnp.bfloat16)
    query_grads = grad_query.reshape(tok_rows, row_width)
    return (log_totals, query_grads, grad_keys, grad_values)


def solution(mesh):
    return jax.shard_map(
        body,
        mesh=mesh,
        in_specs=(
            P("ctx", "head"),
            P("ctx", "head"),
            P("ctx", "head"),
            P("ctx", "head"),
            P("ctx"),
            P(),
            P(),
        ),
        out_specs=(P("ctx", "head"), P("ctx", "head"), P("ctx", "head"), P("ctx", "head")),
        check_vma=False,
    )
```

profile of v0, /device:TPU:13, one launch (start us, length us, event | category | flops | bytes accessed | tf_op | source)
XLA Modules:
  0.0 124.0 jit_solution(4631487437105801853)
XLA Ops:
  0.6 0.0 copy-start.1
  0.6 0.0 copy-start.2
  0.7 0.7 fusion.61
  1.4 0.7 select_reduce_fusion.3
  2.1 1.0 multiply_convert_fusion.1
  3.1 0.2 copy.73
  3.3 0.2 copy.75
  3.5 1.1 copy.72
  4.6 0.2 copy.74
  4.8 0.0 copy-done.1
  4.8 17.1 %all_gather.6 = bf16[2048,128]{1,0:T(8,128)(2,1)S(1)} all-gather(bf16[128,128]{1,0:T(8,128)(2,1)S(1)} %copy-done.1), channel_id=1, replica_groups=mesh['ctx'=16,'head'=2] {'ctx'}, dimensions={0}, use_global_device_ids=true | all-gather | bytes 557056 | tf_op jit(solution)/shard_map/all_gather | solution.py:96
  21.9 0.0 copy-done.2
  21.9 22.8 %all_gather.7 = bf16[2048,128]{1,0:T(8,128)(2,1)S(1)} all-gather(bf16[128,128]{1,0:T(8,128)(2,1)S(1)} %copy-done.2), channel_id=1, replica_groups=mesh['ctx'=16,'head'=2] {'ctx'}, dimensions={0}, use_global_device_ids=true | all-gather | bytes 557056 | tf_op jit(solution)/shard_map/all_gather | solution.py:97
  44.7 0.1 pad_add_fusion
  44.8 3.9 %while.53 = (s32[]{:T(128)}, f32[128,6]{0,1:T(8,128)S(1)}, f32[128,6]{0,1:T(8,128)S(1)}, f32[128,6]{0,1:T(8,128)S(1)}, s32[]{:T(128)}, /*index=5*/s32[]{:T(128)}...) while((s32[]{:T(128)}, f32[128,6]{0,1:T(8,128)S(1)}, ...), condition=%wide.region_15.0_spmd.clone, body=%wide.region_1.15_spmd.clone.sunk | while | flops 205327120 | bytes 6221379 | solution.py:107
  44.8 1.7 %conditional.6 = ((f32[128,6]{0,1:T(8,128)S(1)}, f32[128,6]{0,1:T(8,128)S(1)}, f32[128,6]{0,1:T(8,128)S(1)})) conditional(s32[]{:T(128)} %clamp.18, (f32[128,6]{0,1:T(8,128)S(1)}, f32[128,6]{0,1:T(8,128)S(1)}, f32[128,6]{0,1:T(8,128)S(1)}) %tuple.202, (f32[128,6]{0,1:T(8,128)S(1)}, s32[]{:T(128)}, s32[]{:T(128)}, ...), branch_computations={%region_2.2_spmd, %region_3.6_spmd, %region_7.10_spmd, %region_11.... | conditional | flops 205327104 | bytes 5696036 | solution.py:61
  44.9 0.1 broadcast_compare_fusion.2
  45.0 0.5 select_reduce_fusion.2
  45.4 0.6 multiply_reduce_fusion
  46.0 0.5 fusion.20
  46.6 1.7 %conditional.6 = ((f32[128,6]{0,1:T(8,128)S(1)}, f32[128,6]{0,1:T(8,128)S(1)}, f32[128,6]{0,1:T(8,128)S(1)})) conditional(s32[]{:T(128)} %clamp.18, (f32[128,6]{0,1:T(8,128)S(1)}, f32[128,6]{0,1:T(8,128)S(1)}, f32[128,6]{0,1:T(8,128)S(1)}) %tuple.202, (f32[128,6]{0,1:T(8,128)S(1)}, s32[]{:T(128)}, s32[]{:T(128)}, ...), branch_computations={%region_2.2_spmd, %region_3.6_spmd, %region_7.10_spmd, %region_11.... | conditional | flops 205327104 | bytes 5696036 | solution.py:61
  46.7 0.1 broadcast_compare_fusion.2
  46.8 0.5 select_reduce_fusion.2
  47.3 0.6 multiply_reduce_fusion
  47.8 0.5 fusion.20
  48.7 1.5 %broadcast_in_dim.124.clone = f32[2048,256]{1,0:T(8,128)} broadcast(f32[]{:T(128)} %constant.488.clone.1), dimensions={} | broadcast | bytes 2097156 | tf_op jit(solution)/shard_map/broadcast_in_dim | solution.py:172
  50.2 8.7 %while.54 = (s32[]{:T(128)}, f32[128,6,128]{2,0,1:T(8,128)S(1)}, f32[2048,256]{1,0:T(8,128)}, s32[]{:T(128)}, s32[]{:T(128)}, /*index=5*/bf16[2048,128]{1,0:T(8,...) while((s32[]{:T(128)}, f32[128,6,128]{2,0,1:T(8,128)S(1)}, ...), condition=%wide.region_21.22_spmd.clone, body=%wide.region_16.21_spmd.clone.sunk | while | flops 506528256 | bytes 13381159 | solution.py:168
  50.2 2.1 %conditional.7 = (f32[128,6,128]{2,0,1:T(8,128)S(1)}, f32[512,256]{0,1:T(8,128)S(1)}) conditional(s32[]{:T(128)} %clamp.19, f32[128,6,128]{2,0,1:T(8,128)S(1)} %get-tuple-element.1421, (f32[128,6,128]{2,0,1:T(8,128)S(1)}, s32[]{:T(128)}, s32[]{:T(128)}, bf16[128,6,128]{0,2,1:T(8,128)(2,1)S(1)}, ...), branch_computations={%region_17.17_spmd, %region_18.18_spmd, %region_19.19_spmd, %regio... | conditional | flops 506528256 | bytes 10758676 | solution.py:61
  50.2 0.1 broadcast_compare_fusion.5
  50.4 0.5 exponential_select_fusion.3
  50.9 0.3 convolution_bitcast_fusion.4
  51.2 0.4 multiply_convert_fusion
  51.6 0.3 fusion.56
  51.9 0.4 fusion.55
  52.3 0.2 copy.91
  52.5 0.8 constant_dynamic-update-slice_fusion.2
  53.4 2.1 %conditional.7 = (f32[128,6,128]{2,0,1:T(8,128)S(1)}, f32[512,256]{0,1:T(8,128)S(1)}) conditional(s32[]{:T(128)} %clamp.19, f32[128,6,128]{2,0,1:T(8,128)S(1)} %get-tuple-element.1421, (f32[128,6,128]{2,0,1:T(8,128)S(1)}, s32[]{:T(128)}, s32[]{:T(128)}, bf16[128,6,128]{0,2,1:T(8,128)(2,1)S(1)}, ...), branch_computations={%region_17.17_spmd, %region_18.18_spmd, %region_19.19_spmd, %regio... | conditional | flops 506528256 | bytes 10758676 | solution.py:61
  53.4 0.1 broadcast_compare_fusion.5
  53.5 0.5 exponential_select_fusion.3
  54.1 0.3 convolution_bitcast_fusion.4
  54.3 0.4 multiply_convert_fusion
  54.8 0.3 fusion.56
  55.0 0.4 fusion.55
  55.5 0.2 copy.91
  55.7 0.9 constant_dynamic-update-slice_fusion.2
  56.6 0.1 conditional.7
  56.6 0.1 broadcast.400
  56.7 0.2 copy.91
  56.9 0.9 constant_dynamic-update-slice_fusion.2
  57.7 0.1 conditional.7
  57.8 0.1 broadcast.400
  57.8 0.2 copy.91
  58.1 0.9 constant_dynamic-update-slice_fusion.2
  58.9 0.0 copy-start
  58.9 2.9 %copy.78 = f32[16,128,256]{1,2,0:T(8,128)} copy(f32[16,128,256]{2,1,0:T(8,128)} %bitcast.88) | data formatting | bytes 4194304 | tf_op jit(solution)/shard_map/reshape | solution.py:176
  61.8 0.0 copy-done
  61.8 13.2 %all-to-all-start = ((f32[16,128,256]{1,2,0:T(8,128)}), f32[16,128,256]{1,2,0:T(8,128)S(1)}, u32[]{:S(2)}, u32[]{:S(2)}) async-start(f32[16,128,256]{1,2,0:T(8,128)} %copy.78), calls=%async_computation | async-start | bytes 4194304 | tf_op jit(solution)/shard_map/all_to_all | solution.py:175
  75.0 0.2 copy.76
  75.2 0.9 copy.80
  76.1 46.3 %all-to-all-done = f32[16,128,256]{1,2,0:T(8,128)S(1)} async-done(((f32[16,128,256]{1,2,0:T(8,128)}), f32[16,128,256]{1,2,0:T(8,128)S(1)}, u32[]{:S(2)}, u32[]{:S(2)}) %all-to-all-start) | async-done | bytes 2097184 | tf_op jit(solution)/shard_map/all_to_all | solution.py:175
  122.4 0.1 reduce_sum.73
  122.5 0.7 copy.82
  123.2 0.7 copy.81
  (45 shorter events, 0.5 us)
Async XLA Ops:
  0.6 4.1 %copy-start.1 = (bf16[128,128]{1,0:T(8,128)(2,1)S(1)}, bf16[128,128]{1,0:T(8,128)(2,1)}, u32[]{:S(2)}) copy-start(bf16[128,128]{1,0:T(8,128)(2,1)} %param.52) | copy-start | bytes 98308
  0.6 21.2 %copy-start.2 = (bf16[128,128]{1,0:T(8,128)(2,1)S(1)}, bf16[128,128]{1,0:T(8,128)(2,1)}, u32[]{:S(2)}) copy-start(bf16[128,128]{1,0:T(8,128)(2,1)} %param.53) | copy-start | bytes 98308
  58.9 2.9 %copy-start = (f32[128,6]{0,1:T(8,128)}, f32[128,6]{0,1:T(8,128)S(1)}, u32[]{:S(2)}) copy-start(f32[128,6]{0,1:T(8,128)S(1)} %get-tuple-element.1469) | copy-start | bytes 9220
  61.8 60.6 %all-to-all-start = ((f32[16,128,256]{1,2,0:T(8,128)}), f32[16,128,256]{1,2,0:T(8,128)S(1)}, u32[]{:S(2)}, u32[]{:S(2)}) async-start(f32[16,128,256]{1,2,0:T(8,128)} %copy.78), calls=%async_computation | async-start | bytes 4194304 | tf_op jit(solution)/shard_map/all_to_all | solution.py:175
where the time goes:
time: 124 us
  waiting for transfers between devices  46.3 us (37%)
  blocking collectives  39.9 us (32%)
  starting transfers between devices  13.2 us (11%)
  local copies, waits for them, and re-layouts  13.1 us (11%)
  matrix products  5.79 us (5%)
  other arithmetic  4.14 us (3%)
    all_to_all x1, waiting for transfers between devices, body(): lax.all_to_all(partial_sums.reshape(ctx_count, tok_rows, 2 * head_dim), '...  46.3 us
    all_gather x1, blocking collectives, body(): value_piece = lax.all_gather(value_rows, 'ctx', axis=0, tiled=True)  22.8 us
    all_gather x1, blocking collectives, body(): key_piece = lax.all_gather(key_rows, 'ctx', axis=0, tiled=True)  17.1 us
    all_to_all x1, starting transfers between devices, body(): lax.all_to_all(partial_sums.reshape(ctx_count, tok_rows, 2 * head_dim), '...  13.2 us
    dynamic_update_slice x8, local copies, waits for them, and re-layouts, backward_step(): lax.dynamic_update_slice_in_dim(partial_sums, block_sums, key_start, 0)  4.17 us
    unnamed x12, local copies, waits for them, and re-layouts  3.83 us
    reshape x1, local copies, waits for them, and re-layouts, body(): partial_sums.reshape(ctx_count, tok_rows, 2 * head_dim)  2.89 us
  transfers between devices with their start and end apart: 1, of which 1 were waited for; matrix products, arithmetic and copies ran while one was open for 1% of the time, Pallas kernels for 0%

commit v1 on v0

--- a/solution.py
+++ b/solution.py
@@ -93,8 +93,11 @@
     row_peak = jnp.full((tok_rows, head_count), -1e30, jnp.float32)
     row_total = jnp.zeros((tok_rows, head_count), jnp.float32)
     weighted = jnp.zeros((tok_rows, head_count), jnp.float32)
-    key_piece = lax.all_gather(key_rows, "ctx", axis=0, tiled=True)
-    value_piece = lax.all_gather(value_rows, "ctx", axis=0, tiled=True)
+    key_piece, value_piece = jnp.split(
+        lax.all_gather(jnp.concatenate([key_rows, value_rows], axis=1), "ctx", axis=0, tiled=True),
+        [key_rows.shape[1]],
+        axis=1,
+    )
     piece_rows = key_piece.shape[0]
     block_rows = math.gcd(piece_rows, 512)
 

time: 124 us -> 136 us (1.097)
  blocking collectives: 39.9 us -> 0 us
  waiting for transfers between devices: 46.3 us -> 82.5 us
  between operations: 0.74 us -> 14.1 us
  other arithmetic: 4.14 us -> 5.55 us
    all_gather x2 -> x0, blocking collectives: 39.9 us -> none  [the longest x1 22.8 us: body(): value_piece = lax.all_gather(value_rows, 'ctx', axis=0, tiled=True)]
    all_gather x0 -> x1, waiting for transfers between devices: none -> 36.2 us  [body(): lax.all_gather(jnp.concatenate([key_rows, value_rows], axis=1), 'ctx', ax...]
    concatenate x0 -> x1, other arithmetic: none -> 1.41 us  [body(): jnp.concatenate([key_rows, value_rows], axis=1)]
    unnamed x12 -> x8, local copies, waits for them, and re-layouts: 3.83 us -> 3.82 us
  transfers between devices with their start and end apart: 1 -> 2, of which waited for: 1 -> 2; matrix products, arithmetic and copies ran while one was open for 1% -> 4% of each run, Pallas kernels for 0% -> 0%
where the time goes in v1:
time: 136 us
  waiting for transfers between devices  82.5 us (61%)
  local copies, waits for them, and re-layouts  14.3 us (11%)
  between operations  14.1 us (10%)
  starting transfers between devices  12.6 us (9%)
  matrix products  5.79 us (4%)
  other arithmetic  5.55 us (4%)
    all_to_all x1, waiting for transfers between devices, body(): lax.all_to_all(partial_sums.reshape(ctx_count, tok_rows, 2 * head_dim), '...  46.3 us
    all_gather x1, waiting for transfers between devices, body(): lax.all_gather(jnp.concatenate([key_rows, value_rows], axis=1), 'ctx', ax...  36.2 us
    all_to_all x1, starting transfers between devices, body(): lax.all_to_all(partial_sums.reshape(ctx_count, tok_rows, 2 * head_dim), '...  12.6 us
    dynamic_update_slice x8, local copies, waits for them, and re-layouts, backward_step(): lax.dynamic_update_slice_in_dim(partial_sums, block_sums, key_start, 0)  4.17 us
    unnamed x8, local copies, waits for them, and re-layouts  3.82 us
    reshape x1, local copies, waits for them, and re-layouts, body(): partial_sums.reshape(ctx_count, tok_rows, 2 * head_dim)  2.89 us
  transfers between devices with their start and end apart: 2, of which 2 were waited for; matrix products, arithmetic and copies ran while one was open for 4% of the time, Pallas kernels for 0%

profile of v1, /device:TPU:13, one launch (start us, length us, event | category | flops | bytes accessed | tf_op | source)
XLA Modules:
  0.0 135.8 jit_solution(2724904065656250198)
XLA Ops:
  7.2 0.0 all-gather.2.cloned.1.call-start
  7.2 1.4 %pad_maximum_fusion.3 = bf16[128,256]{1,0:T(8,128)(2,1)} fusion(bf16[128,128]{1,0:T(8,128)(2,1)} %param.53, bf16[128,128]{1,0:T(8,128)(2,1)} %param.52), kind=kLoop, calls=%fused_computation.120 | loop fusion | flops 131072 | bytes 131072 | tf_op jit(solution)/shard_map/concatenate | solution.py:97
  8.6 0.0 all-gather.2.cloned.1.call-update
  8.7 0.7 fusion.61
  9.3 0.7 select_reduce_fusion.3
  10.1 1.0 multiply_convert_fusion.1
  11.1 0.2 copy.73
  11.3 0.2 copy.75
  11.5 1.1 copy.72
  12.6 0.2 copy.74
  12.8 0.1 pad_add_fusion
  12.8 36.2 %all-gather.2.cloned.1.call-done = bf16[2048,256]{1,0:T(8,128)(2,1)} async-done(((bf16[128,256]{1,0:T(8,128)(2,1)}), bf16[2048,256]{1,0:T(8,128)(2,1)}) %all-gather.2.cloned.1.call-update) | async-done | bytes 1048592 | tf_op jit(solution)/shard_map/all_gather | solution.py:97
  49.0 1.3 fusion.62
  50.3 3.9 %while.53 = (s32[]{:T(128)}, f32[128,6]{0,1:T(8,128)S(1)}, f32[128,6]{0,1:T(8,128)S(1)}, f32[128,6]{0,1:T(8,128)S(1)}, s32[]{:T(128)}, /*index=5*/s32[]{:T(128)}...) while((s32[]{:T(128)}, f32[128,6]{0,1:T(8,128)S(1)}, ...), condition=%wide.region_15.0_spmd.clone, body=%wide.region_1.15_spmd.clone.sunk | while | flops 205327120 | bytes 6221379 | solution.py:110
  50.4 1.7 %conditional.6 = ((f32[128,6]{0,1:T(8,128)S(1)}, f32[128,6]{0,1:T(8,128)S(1)}, f32[128,6]{0,1:T(8,128)S(1)})) conditional(s32[]{:T(128)} %clamp.18, (f32[128,6]{0,1:T(8,128)S(1)}, f32[128,6]{0,1:T(8,128)S(1)}, f32[128,6]{0,1:T(8,128)S(1)}) %tuple.203, (f32[128,6]{0,1:T(8,128)S(1)}, s32[]{:T(128)}, s32[]{:T(128)}, ...), branch_computations={%region_2.2_spmd, %region_3.6_spmd, %region_7.10_spmd, %region_11.... | conditional | flops 205327104 | bytes 5696036 | solution.py:61
  50.5 0.1 broadcast_compare_fusion.2
  50.6 0.5 select_reduce_fusion.2
  51.0 0.6 multiply_reduce_fusion
  51.6 0.5 fusion.20
  52.2 1.7 %conditional.6 = ((f32[128,6]{0,1:T(8,128)S(1)}, f32[128,6]{0,1:T(8,128)S(1)}, f32[128,6]{0,1:T(8,128)S(1)})) conditional(s32[]{:T(128)} %clamp.18, (f32[128,6]{0,1:T(8,128)S(1)}, f32[128,6]{0,1:T(8,128)S(1)}, f32[128,6]{0,1:T(8,128)S(1)}) %tuple.203, (f32[128,6]{0,1:T(8,128)S(1)}, s32[]{:T(128)}, s32[]{:T(128)}, ...), branch_computations={%region_2.2_spmd, %region_3.6_spmd, %region_7.10_spmd, %region_11.... | conditional | flops 205327104 | bytes 5696036 | solution.py:61
  52.3 0.1 broadcast_compare_fusion.2
  52.4 0.5 select_reduce_fusion.2
  52.9 0.6 multiply_reduce_fusion
  53.4 0.5 fusion.20
  54.3 1.5 %broadcast_in_dim.124.clone = f32[2048,256]{1,0:T(8,128)} broadcast(f32[]{:T(128)} %constant.488.clone.1), dimensions={} | broadcast | bytes 2097156 | tf_op jit(solution)/shard_map/broadcast_in_dim | solution.py:175
  55.8 8.7 %while.54 = (s32[]{:T(128)}, f32[128,6,128]{2,0,1:T(8,128)S(1)}, f32[2048,256]{1,0:T(8,128)}, s32[]{:T(128)}, s32[]{:T(128)}, /*index=5*/bf16[2048,128]{1,0:T(8,...) while((s32[]{:T(128)}, f32[128,6,128]{2,0,1:T(8,128)S(1)}, ...), condition=%wide.region_21.22_spmd.clone, body=%wide.region_16.21_spmd.clone.sunk | while | flops 506528256 | bytes 13381159 | solution.py:171
  55.8 2.1 %conditional.7 = (f32[128,6,128]{2,0,1:T(8,128)S(1)}, f32[512,256]{0,1:T(8,128)S(1)}) conditional(s32[]{:T(128)} %clamp.19, f32[128,6,128]{2,0,1:T(8,128)S(1)} %get-tuple-element.1423, (f32[128,6,128]{2,0,1:T(8,128)S(1)}, s32[]{:T(128)}, s32[]{:T(128)}, bf16[128,6,128]{0,2,1:T(8,128)(2,1)S(1)}, ...), branch_computations={%region_17.17_spmd, %region_18.18_spmd, %region_19.19_spmd, %regio... | conditional | flops 506528256 | bytes 10758676 | solution.py:61
  55.8 0.1 broadcast_compare_fusion.5
  56.0 0.5 exponential_select_fusion.3
  56.5 0.3 convolution_bitcast_fusion.4
  56.8 0.4 multiply_convert_fusion
  57.2 0.3 fusion.56
  57.5 0.4 fusion.55
  57.9 0.2 copy.91
  58.1 0.8 constant_dynamic-update-slice_fusion.2
  59.0 2.1 %conditional.7 = (f32[128,6,128]{2,0,1:T(8,128)S(1)}, f32[512,256]{0,1:T(8,128)S(1)}) conditional(s32[]{:T(128)} %clamp.19, f32[128,6,128]{2,0,1:T(8,128)S(1)} %get-tuple-element.1423, (f32[128,6,128]{2,0,1:T(8,128)S(1)}, s32[]{:T(128)}, s32[]{:T(128)}, bf16[128,6,128]{0,2,1:T(8,128)(2,1)S(1)}, ...), branch_computations={%region_17.17_spmd, %region_18.18_spmd, %region_19.19_spmd, %regio... | conditional | flops 506528256 | bytes 10758676 | solution.py:61
  59.0 0.1 broadcast_compare_fusion.5
  59.1 0.5 exponential_select_fusion.3
  59.7 0.3 convolution_bitcast_fusion.4
  59.9 0.4 multiply_convert_fusion
  60.4 0.3 fusion.56
  60.6 0.4 fusion.55
  61.1 0.2 copy.91
  61.3 0.9 constant_dynamic-update-slice_fusion.2
  62.1 0.1 conditional.7
  62.2 0.1 broadcast.400
  62.3 0.2 copy.91
  62.5 0.9 constant_dynamic-update-slice_fusion.2
  63.3 0.1 conditional.7
  63.4 0.1 broadcast.400
  63.4 0.2 copy.91
  63.6 0.9 constant_dynamic-update-slice_fusion.2
  64.5 0.0 copy-start
  64.5 2.9 %copy.78 = f32[16,128,256]{1,2,0:T(8,128)} copy(f32[16,128,256]{2,1,0:T(8,128)} %bitcast.88) | data formatting | bytes 4194304 | tf_op jit(solution)/shard_map/reshape | solution.py:179
  67.4 0.0 copy-done
  67.4 12.6 %all-to-all-start = ((f32[16,128,256]{1,2,0:T(8,128)}), f32[16,128,256]{1,2,0:T(8,128)S(1)}, u32[]{:S(2)}, u32[]{:S(2)}) async-start(f32[16,128,256]{1,2,0:T(8,128)} %copy.78), calls=%async_computation | async-start | bytes 4194304 | tf_op jit(solution)/shard_map/all_to_all | solution.py:178
  80.0 0.2 copy.76
  80.1 0.9 copy.80
  81.1 46.3 %all-to-all-done = f32[16,128,256]{1,2,0:T(8,128)S(1)} async-done(((f32[16,128,256]{1,2,0:T(8,128)}), f32[16,128,256]{1,2,0:T(8,128)S(1)}, u32[]{:S(2)}, u32[]{:S(2)}) %all-to-all-start) | async-done | bytes 2097184 | tf_op jit(solution)/shard_map/all_to_all | solution.py:178
  127.4 0.1 reduce_sum.73
  127.5 0.7 copy.82
  128.2 0.7 copy.81
  (45 shorter events, 0.5 us)
Async XLA Ops:
  7.2 41.9 %all-gather.2.cloned.1.call-start = ((), (), s32[]{:S(2)}) async-start(), calls=%async_computation.1 | async-start | bytes 1114112 | tf_op jit(solution)/shard_map/all_gather | solution.py:97
  64.5 2.9 %copy-start = (f32[128,6]{0,1:T(8,128)}, f32[128,6]{0,1:T(8,128)S(1)}, u32[]{:S(2)}) copy-start(f32[128,6]{0,1:T(8,128)S(1)} %get-tuple-element.1475) | copy-start | bytes 9220
  67.4 60.0 %all-to-all-start = ((f32[16,128,256]{1,2,0:T(8,128)}), f32[16,128,256]{1,2,0:T(8,128)S(1)}, u32[]{:S(2)}, u32[]{:S(2)}) async-start(f32[16,128,256]{1,2,0:T(8,128)} %copy.78), calls=%async_computation | async-start | bytes 4194304 | tf_op jit(solution)/shard_map/all_to_all | solution.py:178
Sparse Core Ops, SparseCore 0:
  10.7 38.2 all-gather.1
